TPU v7x, 32 devices: a whole 2x2x4 slice. The times are simulated.
32 devices in a mesh: expert: 4 (over y, x), dp: 8 (over z, core).
Axes of the slice: x: 2, y: 2, z: 4, core: 2. Of those that a mesh axis runs over, the one named last changes fastest.
Arguments:
- routes: int32 [4096, 2], P(('expert', 'dp')), may hold values from 0 to 1, as said below
- expert_inputs: bfloat16 [8, 4, 512, 2048], P('dp', 'expert'), may hold values from -6 to 6
- hidden_grad: bfloat16 [8, 4, 512, 2048], P('dp', 'expert'), may hold values from -6 to 6
- weight: float32 [2048, 8192], P('dp', 'expert'), may hold values from -0.125 to 0.125
- moment_one: float32 [2048, 8192], P('dp', 'expert'), may hold values from -6 to 6
- moment_two: float32 [2048, 8192], P('dp', 'expert'), may hold values from 0.5 to 4
Outputs:
- token_grad: bfloat16 [4096, 2048], P(('expert', 'dp'))
- new_weight: float32 [2048, 8192], P('dp', 'expert')
- new_first: float32 [2048, 8192], P('dp', 'expert')
- new_second: float32 [2048, 8192], P('dp', 'expert')
Inputs may be any that keep to these rules, and one draw needn't show every extreme that they name: `routes`: each token names 2 different experts; the tokens of one device name one expert at most 128 times, and in every device's tokens some expert is named exactly 128 times.
All inputs are finite; a program needn't handle non-finite values.
Results may differ from a plain program's by a relative error of at most 0.0045.
The roundings to bfloat16 on the way count: a program that leaves them out, or rounds other values in their place, can miss the bound.
Values may be sent and summed in bfloat16 or wider, within the bound.
No kernel may reach another device: no remote copies, remote signals or barrier semaphores. Data moves between devices by JAX's collectives and lax.ppermute only.
A program may use at most 128 MiB of HBM per device.

v0:
```python
import jax
import jax.numpy as jnp
from jax import lax
from jax.sharding import PartitionSpec as P

beta_one = 0.9
beta_two = 0.95
learn_rate = 0.003
decay = 0.1
epsilon = 1e-08
loss_scale = 64.0
bias_one = 1.0 - (0.9**50) ** 2
bias_two = 1.0 - (0.95**50) ** 2


def adamw(weight, moment_one, moment_two, grad):
    new_first = beta_one * moment_one + (1.0 - beta_one) * grad
    new_second = beta_two * moment_two + (1.0 - beta_two) * grad * grad
    update = new_first / bias_one / (jnp.sqrt(new_second / bias_two) + epsilon)
    new_weight = weight - learn_rate * (update + decay * weight)
    return (new_weight, new_first, new_second)


def shards(routes, expert_inputs, hidden_grad, weight, moment_one, moment_two):
    n_expert = lax.axis_size("expert")
    experts = n_expert // 2
    slot_rows = expert_inputs.shape[2]
    capacity = slot_rows // n_expert
    width = expert_inputs.shape[3]
    tok_count = routes.shape[0]
    top_count = routes.shape[1]
    flat_routes = routes.reshape(-1)
    onehot = (flat_routes[:, None] == jnp.arange(experts, dtype=jnp.int32)[None, :]).astype(
        jnp.int32
    )
    running = jnp.cumsum(onehot, axis=0)
    slots = jnp.sum((running - 1) * onehot, axis=1).reshape(tok_count, top_count)
    counts = jnp.sum(onehot, axis=0)
    all_counts = lax.all_gather(counts[None, :], "expert", axis=0, tiled=True)
    my_expert = lax.axis_index("expert") // 2
    chosen = jnp.arange(experts, dtype=jnp.int32)[None, :] == my_expert
    my_counts = jnp.sum(jnp.where(chosen, all_counts, 0), axis=1)
    valid = (jnp.arange(capacity, dtype=jnp.int32)[None, :] < my_counts[:, None]).reshape(-1)
    inputs_flat = expert_inputs.reshape(slot_rows, width)
    grad_flat = hidden_grad.reshape(slot_rows, -1)
    masked = jnp.where(valid[:, None], grad_flat, jnp.zeros_like(grad_flat))
    wbf = weight.astype(jnp.bfloat16)
    partial_rows = lax.dot_general(
        masked,
        lax.all_gather(wbf, "dp", axis=0, tiled=True),
        (((1,), (1,)), ((), ())),
        preferred_element_type=jnp.float32,
    )
    sent = partial_rows.reshape(n_expert, capacity, width)
    received = lax.all_to_all(sent, "expert", split_axis=0, concat_axis=0, tiled=True)
    paired = jnp.sum(received.reshape(experts, 2, capacity, width), axis=1).astype(jnp.bfloat16)
    picked = paired[routes, slots]
    token_grad = jnp.sum(picked.astype(jnp.float32), axis=1).astype(jnp.bfloat16)
    owned = lax.psum_scatter(
        lax.dot_general(
            inputs_flat, masked, (((0,), (0,)), ((), ())), preferred_element_type=jnp.float32
        ).astype(jnp.bfloat16),
        "dp",
        scatter_dimension=0,
        tiled=True,
    ).astype(jnp.float32)
    new_weight, new_first, new_second = adamw(weight, moment_one, moment_two, owned / loss_scale)
    return (token_grad, new_weight, new_first, new_second)


def solution(mesh):
    in_specs = (
        P(("expert", "dp"), None),
        P("dp", "expert", None, None),
        P("dp", "expert", None, None),
        P("dp", "expert"),
        P("dp", "expert"),
        P("dp", "expert"),
    )
    out_specs = (P(("expert", "dp"), None), P("dp", "expert"), P("dp", "expert"), P("dp", "expert"))
    return jax.shard_map(shards, mesh=mesh, in_specs=in_specs, out_specs=out_specs, check_vma=False)
```

profile of v0, /device:TPU:0, one launch (start us, length us, event | category | flops | bytes accessed | tf_op | source)
XLA Modules:
  0.0 221.4 jit_solution(1023216353679421165)
XLA Ops:
  7.2 0.0 copy-start
  7.2 0.0 copy-start.2
  7.2 0.0 copy-start.1
  7.2 0.0 all-gather.3.cloned.1.call-start
  7.2 2.9 %convert_element_type.25 = bf16[256,2048]{1,0:T(8,128)(2,1)} convert(f32[256,2048]{1,0:T(8,128)} %param.9) | non-fusion elementwise | flops 524288 | bytes 3145728 | tf_op jit(solution)/shard_map/convert_element_type | solution.py:47
  10.1 0.0 all-gather.3.cloned.1.call-update
  10.1 0.0 reduce-scatter.2.cloned.1.call-start
  10.2 0.0 copy-done.1
  10.2 0.1 copy.31
  10.3 0.1 eq.42
  10.4 0.1 eq.38
  10.6 0.6 reduce-window.6
  11.2 0.2 slice_reduce_fusion
  11.4 0.2 reduce-window.9
  11.6 0.0 copy-done.2
  11.6 0.6 dynamic-slice
  12.9 0.1 add_bitcast_fusion
  12.9 0.1 fusion.14
  13.1 0.2 dynamic-update-slice
  13.3 8.8 %all-reduce = s32[8]{0:T(128)S(1)} all-reduce(s32[8]{0:T(128)S(1)} %dynamic-update-slice), channel_id=2, replica_groups=mesh['expert'=4,'dp'=8] {'expert'}, use_global_device_ids=true, to_apply=%add | all-reduce | flops 8 | bytes 64
  22.1 0.1 reshape.114
  22.2 0.1 select_reduce_fusion
  22.3 0.1 fusion.23
  22.4 0.0 copy-done
  22.4 8.8 %convert_bitcast_fusion = bf16[2048,2048]{0,1:T(8,128)(2,1)} fusion(bf16[1,1,512,2048]{3,2,1,0:T(8,128)(2,1)S(1)} %copy-done, bf16[1,1,512,2048]{3,2,1,0:T(8,128)(2,1)} %param.8, pred[512]{0:T(512)(128)(4,1)S(1)} %get-tuple-element.21), kind=kOutput, calls=%fused_computation.3 | convolution fusion | flops 4300210176 | bytes 12583424 | tf_op jit(solution)/shard_map/dot_general | solution.py:60
  31.2 0.0 reduce-scatter.2.cloned.1.call-update
  31.2 63.8 %all-gather.3.cloned.1.call-done = bf16[2048,2048]{1,0:T(8,128)(2,1)} async-done(((bf16[256,2048]{1,0:T(8,128)(2,1)}), bf16[2048,2048]{1,0:T(8,128)(2,1)}) %all-gather.3.cloned.1.call-update) | async-done | bytes 8388624 | tf_op jit(solution)/shard_map/all_gather | solution.py:50
  95.0 10.5 %fusion = f32[4,128,2048]{2,1,0:T(8,128)} fusion(bf16[2048,2048]{1,0:T(8,128)(2,1)} %all-gather.3.cloned.1.call-done, bf16[4,128,2048]{2,1,0:T(8,128)(2,1)} %bitcast.39, pred[4,128]{1,0:T(4,128)(4,1)S(1)} %get-tuple-element.22), kind=kOutput, calls=%fused_computation.1 | convolution fusion | flops 4296015872 | bytes 14680576 | tf_op jit(solution)/shard_map/dot_general | solution.py:48
  105.6 5.1 %all-to-all-start = ((f32[4,128,2048]{2,1,0:T(8,128)}), f32[4,128,2048]{2,1,0:T(8,128)}, u32[]{:S(2)}, u32[]{:S(2)}) async-start(f32[4,128,2048]{2,1,0:T(8,128)} %fusion), calls=%async_computation | async-start | bytes 8388608 | tf_op jit(solution)/shard_map/all_to_all | solution.py:55
  110.7 2.9 %copy.40 = f32[256,2048]{0,1:T(8,128)} copy(f32[256,2048]{1,0:T(8,128)} %param.9) | data formatting | bytes 4194304 | tf_op args[3]
  113.6 0.1 reshape.106
  113.7 0.1 copy.33
  113.8 0.1 copy.36
  113.9 0.1 reshape.108
  114.1 2.9 %copy.37 = f32[256,2048]{0,1:T(8,128)} copy(f32[256,2048]{1,0:T(8,128)} %param.10) | data formatting | bytes 4194304 | tf_op args[4]
  117.0 2.9 %copy.38 = f32[256,2048]{0,1:T(8,128)} copy(f32[256,2048]{1,0:T(8,128)} %param.11) | data formatting | bytes 4194304 | tf_op args[5]
  119.9 65.6 %reduce-scatter.2.cloned.1.call-done = bf16[256,2048]{0,1:T(8,128)(2,1)} async-done(((bf16[2048,2048]{0,1:T(8,128)(2,1)}), bf16[256,2048]{0,1:T(8,128)(2,1)}) %reduce-scatter.2.cloned.1.call-update) | async-done | bytes 1048592 | tf_op jit(solution)/shard_map/reduce_scatter | solution.py:59
  185.5 7.0 %multiply_subtract_fusion = (f32[256,2048]{0,1:T(8,128)}, f32[256,2048]{0,1:T(8,128)}, f32[256,2048]{0,1:T(8,128)}) fusion(f32[256,2048]{0,1:T(8,128)} %copy.40, bf16[256,2048]{0,1:T(8,128)(2,1)} %reduce-scatter.2.cloned.1.call-done, f32[256,2048]{0,1:T(8,128)} %copy.37, f32[256,2048]{0,1:T(8,128)} %copy.38), kind=kLoop, calls=%fused_computation.13 | loop fusion | flops 8912896 | bytes 13631488 | tf_op jit(solution)/shard_map/sub | solution.py:20
  192.5 2.9 %copy.41 = f32[256,2048]{1,0:T(8,128)} copy(f32[256,2048]{0,1:T(8,128)} %get-tuple-element.18) | data formatting | bytes 4194304
  195.4 2.9 %copy.42 = f32[256,2048]{1,0:T(8,128)} copy(f32[256,2048]{0,1:T(8,128)} %get-tuple-element.19) | data formatting | bytes 4194304
  198.2 2.9 %copy.43 = f32[256,2048]{1,0:T(8,128)} copy(f32[256,2048]{0,1:T(8,128)} %get-tuple-element.20) | data formatting | bytes 4194304
  201.1 0.0 all-to-all-done
  201.1 2.7 %bitcast_reduce_fusion = bf16[2,128,2048]{2,1,0:T(8,128)(2,1)S(1)} fusion(f32[4,128,2048]{2,1,0:T(8,128)} %all-to-all-done), kind=kLoop, calls=%fused_computation.4 | loop fusion | flops 524288 | bytes 5242880 | tf_op jit(solution)/shard_map/reduce_sum | solution.py:56
  203.9 5.3 %gather_fusion = bf16[256,2048]{1,0:T(8,128)(2,1)} fusion(bf16[2,128,2048]{2,1,0:T(8,128)(2,1)S(1)} %bitcast_reduce_fusion, s32[256]{0:T(256)S(1)} %reshape.108), kind=kCustom, calls=%fused_computation | custom fusion | bytes 2099200 | tf_op jit(solution)/shard_map/gather | solution.py:57
  209.2 1.7 reshape.111
  210.9 3.6 %reduce_sum.52 = bf16[128,2048]{1,0:T(8,128)(2,1)} reduce(bf16[128,2,2048]{2,1,0:T(2,128)(2,1)S(1)} %reshape.111, bf16[]{:T(256)} %constant.46.clone.1), dimensions={1}, to_apply=%region_6.7 | reduce | flops 262144 | bytes 1572866 | tf_op jit(solution)/shard_map/reduce_sum | solution.py:58
  (4 shorter events, 0.0 us)
Async XLA Ops:
  7.2 15.2 %copy-start = (bf16[1,1,512,2048]{3,2,1,0:T(8,128)(2,1)S(1)}, bf16[1,1,512,2048]{3,2,1,0:T(8,128)(2,1)}, u32[]{:S(2)}) copy-start(bf16[1,1,512,2048]{3,2,1,0:T(8,128)(2,1)} %param.7) | copy-start | bytes 6291460
  7.2 4.4 %copy-start.2 = (u32[32]{0:T(128)S(1)}, u32[32]{0:T(128)}, u32[]{:S(2)}) copy-start(u32[32]{0:T(128)} %constant.77) | copy-start | bytes 388
  7.2 3.0 %copy-start.1 = (s32[128,2]{0,1:T(2,128)S(1)}, s32[128,2]{0,1:T(2,128)}, u32[]{:S(2)}) copy-start(s32[128,2]{0,1:T(2,128)} %param.6) | copy-start | bytes 3076
  7.2 87.8 %all-gather.3.cloned.1.call-start = ((), (), s32[]{:S(2)}) async-start(), calls=%async_computation.2 | async-start | bytes 9437184 | tf_op jit(solution)/shard_map/all_gather | solution.py:50
  10.1 175.4 %reduce-scatter.2.cloned.1.call-start = ((), (), s32[]{:S(2)}) async-start(), calls=%async_computation.3 | async-start | bytes 9437184 | tf_op jit(solution)/shard_map/reduce_scatter | solution.py:59
  105.6 95.5 %all-to-all-start = ((f32[4,128,2048]{2,1,0:T(8,128)}), f32[4,128,2048]{2,1,0:T(8,128)}, u32[]{:S(2)}, u32[]{:S(2)}) async-start(f32[4,128,2048]{2,1,0:T(8,128)} %fusion), calls=%async_computation | async-start | bytes 8388608 | tf_op jit(solution)/shard_map/all_to_all | solution.py:55
Sparse Core Ops, SparseCore 0:
  10.2 84.7 all-gather.2
  97.3 88.1 reduce-scatter.1
where the time goes:
time: 222 us; the launch traced here: 221 us
  waiting for transfers between devices  129 us (58%)
  local copies, waits for them, and re-layouts  26.4 us (12%)
  matrix products  19.4 us (9%)
  other arithmetic  17.4 us (8%)
  between operations  14.8 us (7%)
  blocking collectives  8.82 us (4%)
  starting transfers between devices  5.2 us (2%)
    reduce_scatter x1, waiting for transfers between devices, shards(): lax.psum_scatter(lax.dot_general(inputs_flat, masked, (((0,), (0,)), ((),...  65.6 us
    all_gather x1, waiting for transfers between devices, shards(): lax.all_gather(wbf, 'dp', axis=0, tiled=True)  63.8 us
    unnamed x16, local copies, waits for them, and re-layouts  18.3 us
    dot_general x1, matrix products, shards(): lax.dot_general(masked, lax.all_gather(wbf, 'dp', axis=0, tiled=True), ((...  10.5 us
    unnamed x1, blocking collectives  8.82 us
    dot_general x1, matrix products, shards(): lax.dot_general(inputs_flat, masked, (((0,), (0,)), ((), ())), preferred_...  8.81 us
    gather x2, local copies, waits for them, and re-layouts, shards(): picked = paired[routes, slots]  7.06 us
    sub x1, other arithmetic, adamw(): new_weight = weight - learn_rate * (update + decay * weight)  6.97 us
  transfers between devices with their start and end apart: 3, of which 2 were waited for; matrix products, arithmetic and copies ran while one was open for 21% of the time, Pallas kernels for 0%

commit v1 on v0

--- a/solution.py
+++ b/solution.py
@@ -11,6 +11,18 @@
 loss_scale = 64.0
 bias_one = 1.0 - (0.9**50) ** 2
 bias_two = 1.0 - (0.95**50) ** 2
+
+
+def gather_by_bits(value, axis, dim):
+    ways, here, step = (lax.axis_size(axis), lax.axis_index(axis), value.shape[dim])
+    line, have = (value, 1)
+    while have < ways:
+        line = jnp.concatenate(
+            [line, lax.ppermute(line, axis, [(d, (d - have) % ways) for d in range(ways)])],
+            axis=dim,
+        )
+        have = 2 * have
+    return jnp.roll(line, here * step, axis=dim)
 
 
 def adamw(weight, moment_one, moment_two, grad):
@@ -47,7 +59,7 @@
     wbf = weight.astype(jnp.bfloat16)
     partial_rows = lax.dot_general(
         masked,
-        lax.all_gather(wbf, "dp", axis=0, tiled=True),
+        gather_by_bits(wbf, "dp", 0),
         (((1,), (1,)), ((), ())),
         preferred_element_type=jnp.float32,
     )

time: 222 us -> 462 us (2.08)
  waiting for transfers between devices: 129 us -> 353 us
  local copies, waits for them, and re-layouts: 26.4 us -> 41.2 us
    ppermute x0 -> x3, waiting for transfers between devices: none -> 312 us  [gather_by_bits(): lax.ppermute(line, axis, [(d, (d - have) % ways) for d in range(ways)])]
    reduce_scatter x1, waiting for transfers between devices: 65.6 us -> 0.01 us  [shards(): lax.psum_scatter(lax.dot_general(inputs_flat, masked, (((0,), (0,)), ((),...]
    all_gather x1 -> x0, waiting for transfers between devices: 63.8 us -> none  [shards(): lax.all_gather(wbf, 'dp', axis=0, tiled=True)]
    all_to_all x1, waiting for transfers between devices: 0.01 us -> 40.6 us  [shards(): lax.all_to_all(sent, 'expert', split_axis=0, concat_axis=0, tiled=True)]
    unnamed x16 -> x38, local copies, waits for them, and re-layouts: 18.3 us -> 29.4 us
    concatenate x0 -> x1, local copies, waits for them, and re-layouts: none -> 4.88 us  [gather_by_bits(): return jnp.roll(line, here * step, axis=dim)]
  transfers between devices with their start and end apart: 3 -> 5, of which waited for: 2 -> 4; matrix products, arithmetic and copies ran while one was open for 21% -> 11% of each run, Pallas kernels for 0% -> 0%
where the time goes in v1:
time: 462 us; the launch traced here: 461 us
  waiting for transfers between devices  353 us (76%)
  local copies, waits for them, and re-layouts  41.2 us (9%)
  other arithmetic  18.5 us (4%)
  matrix products  18.2 us (4%)
  between operations  14.8 us (3%)
  blocking collectives  8.82 us (2%)
  starting transfers between devices  6.87 us (1%)
    ppermute x3, waiting for transfers between devices, gather_by_bits(): lax.ppermute(line, axis, [(d, (d - have) % ways) for d in range(ways)])  312 us
    all_to_all x1, waiting for transfers between devices, shards(): lax.all_to_all(sent, 'expert', split_axis=0, concat_axis=0, tiled=True)  40.6 us
    unnamed x38, local copies, waits for them, and re-layouts  29.4 us
    dot_general x1, matrix products, shards(): lax.dot_general(masked, gather_by_bits(wbf, 'dp', 0), (((1,), (1,)), ((),...  9.56 us
  transfers between devices with their start and end apart: 5, of which 4 were waited for; matrix products, arithmetic and copies ran while one was open for 11% of the time, Pallas kernels for 0%

profile of v1, /device:TPU:0, one launch (start us, length us, event | category | flops | bytes accessed | tf_op | source)
XLA Modules:
  0.0 461.2 jit_solution(18134090466026768931)
XLA Ops:
  7.2 0.9 copy.31
  8.2 0.1 eq.45
  8.3 0.1 eq.41
  8.5 0.6 reduce-window.6
  9.1 0.2 slice_reduce_fusion
  9.3 0.2 reduce-window.9
  9.5 0.1 add_bitcast_fusion
  9.6 0.1 fusion.15
  9.7 1.2 dynamic-slice
  11.6 0.2 dynamic-update-slice
  11.8 8.8 %all-reduce = s32[8]{0:T(128)S(1)} all-reduce(s32[8]{0:T(128)S(1)} %dynamic-update-slice), channel_id=2, replica_groups=mesh['expert'=4,'dp'=8] {'expert'}, use_global_device_ids=true, to_apply=%add | all-reduce | flops 8 | bytes 64
  20.6 0.1 reshape.114
  20.7 0.1 select_reduce_fusion
  20.9 0.1 fusion.25
  20.9 8.7 %convert_bitcast_fusion = bf16[2048,2048]{0,1:T(8,128)(2,1)} fusion(bf16[1,1,512,2048]{3,2,1,0:T(8,128)(2,1)S(1)} %copy-done, bf16[1,1,512,2048]{3,2,1,0:T(8,128)(2,1)} %param.8, pred[512]{0:T(512)(128)(4,1)S(1)} %get-tuple-element.23), kind=kOutput, calls=%fused_computation.3 | convolution fusion | flops 4300210176 | bytes 12583424 | tf_op jit(solution)/shard_map/dot_general | solution.py:72
  29.6 1.6 copy-done.4
  31.2 1.2 constant_dynamic-update-slice_fusion.7
  32.3 1.0 collective-permute-start
  33.4 31.8 %collective-permute-done = bf16[256,2048]{1,0:T(8,128)(2,1)S(1)} collective-permute-done((bf16[256,2048]{1,0:T(8,128)(2,1)S(1)}, bf16[256,2048]{1,0:T(8,128)(2,1)S(1)}, u32[]{:S(2)}, u32[]{:S(2)}) %collective-permute-start) | collective-permute-done | bytes 1048608 | tf_op jit(solution)/shard_map/ppermute | solution.py:21
  65.2 0.2 pad_maximum_fusion.1
  65.4 0.6 collective-permute-start.1
  66.0 92.1 %collective-permute-done.1 = bf16[512,2048]{1,0:T(8,128)(2,1)S(1)} collective-permute-done((bf16[512,2048]{1,0:T(8,128)(2,1)S(1)}, bf16[512,2048]{1,0:T(8,128)(2,1)S(1)}, u32[]{:S(2)}, u32[]{:S(2)}) %collective-permute-start.1) | collective-permute-done | bytes 2097184 | tf_op jit(solution)/shard_map/ppermute | solution.py:21
  158.1 2.3 pad_maximum_fusion
  160.4 1.1 constant_dynamic-update-slice_fusion.6
  161.5 1.4 constant_dynamic-update-slice_fusion.5
  163.0 188.2 %collective-permute-done.2 = bf16[1024,2048]{1,0:T(8,128)(2,1)} collective-permute-done((bf16[1024,2048]{1,0:T(8,128)(2,1)}, bf16[1024,2048]{1,0:T(8,128)(2,1)}, u32[]{:S(2)}, u32[]{:S(2)}) %collective-permute-start.2) | collective-permute-done | bytes 4194336 | tf_op jit(solution)/shard_map/ppermute | solution.py:21
  351.2 4.7 %constant_dynamic-update-slice_fusion.4 = bf16[4096,2048]{1,0:T(8,128)(2,1)} fusion(bf16[4096,2048]{1,0:T(8,128)(2,1)} %constant_dynamic-update-slice_fusion.5, bf16[1024,2048]{1,0:T(8,128)(2,1)} %collective-permute-done.2), kind=kLoop, calls=%fused_computation.27 | loop fusion | bytes 8388608
  355.9 1.1 constant_dynamic-update-slice_fusion.3
  357.1 1.0 constant_dynamic-update-slice_fusion.2
  358.1 1.4 constant_dynamic-update-slice_fusion.1
  359.5 4.9 %constant_dynamic-update-slice_fusion = bf16[4096,2048]{1,0:T(8,128)(2,1)} fusion(bf16[4096,2048]{1,0:T(8,128)(2,1)} %constant_dynamic-update-slice_fusion.1, bf16[1024,2048]{1,0:T(8,128)(2,1)} %collective-permute-done.2), kind=kLoop, calls=%fused_computation.23 | loop fusion | bytes 8388608 | tf_op jit(solution)/shard_map/jit(_roll_dynamic)/concatenate | solution.py:25
  364.4 9.6 %fusion = f32[4,128,2048]{2,1,0:T(8,128)} fusion(bf16[4096,2048]{1,0:T(8,128)(2,1)} %constant_dynamic-update-slice_fusion, s32[]{:T(128)S(6)} %select_n.48, bf16[4,128,2048]{2,1,0:T(8,128)(2,1)S(1)} %bitcast.39, pred[4,128]{1,0:T(4,128)(4,1)S(1)} %get-tuple-element.24), kind=kOutput, calls=%fused_computation.1 | convolution fusion | flops 4296015872 | bytes 14680580 | tf_op jit(solution)/shard_map/dot_general | solution.py:60
  374.0 5.2 %all-to-all-start = ((f32[4,128,2048]{2,1,0:T(8,128)}), f32[4,128,2048]{2,1,0:T(8,128)}, u32[]{:S(2)}, u32[]{:S(2)}) async-start(f32[4,128,2048]{2,1,0:T(8,128)} %fusion), calls=%async_computation | async-start | bytes 8388608 | tf_op jit(solution)/shard_map/all_to_all | solution.py:67
  379.2 1.8 copy.40
  381.0 0.1 reshape.106
  381.2 0.1 copy.36
  381.3 0.1 reshape.108
  381.5 3.0 copy.37
  384.5 1.8 copy.38
  386.3 40.6 %all-to-all-done = f32[4,128,2048]{2,1,0:T(8,128)} async-done(((f32[4,128,2048]{2,1,0:T(8,128)}), f32[4,128,2048]{2,1,0:T(8,128)}, u32[]{:S(2)}, u32[]{:S(2)}) %all-to-all-start) | async-done | bytes 4194336 | tf_op jit(solution)/shard_map/all_to_all | solution.py:67
  426.9 2.7 bitcast_reduce_fusion
  429.7 4.3 gather_fusion
  434.0 1.6 reshape.111
  435.6 4.6 reduce_sum.52
  440.2 6.3 %multiply_subtract_fusion = (f32[256,2048]{0,1:T(8,128)}, f32[256,2048]{0,1:T(8,128)}, f32[256,2048]{0,1:T(8,128)}) fusion(f32[256,2048]{0,1:T(8,128)S(1)} %copy-done.6, bf16[256,2048]{0,1:T(8,128)(2,1)} %reduce-scatter.2.cloned.1.call-done, f32[256,2048]{0,1:T(8,128)} %copy.37, f32[256,2048]{0,1:T(8,128)} %copy.38), kind=kLoop, calls=%fused_computation.16 | loop fusion | flops 8912896 | bytes 13631488 | tf_op jit(solution)/shard_map/sub | solution.py:32
  446.5 3.0 copy.41
  449.5 1.8 copy.42
  451.3 3.0 copy.43
  (30 shorter events, 0.2 us)
Async XLA Ops:
  7.2 13.8 %copy-start = (bf16[1,1,512,2048]{3,2,1,0:T(8,128)(2,1)S(1)}, bf16[1,1,512,2048]{3,2,1,0:T(8,128)(2,1)}, u32[]{:S(2)}) copy-start(bf16[1,1,512,2048]{3,2,1,0:T(8,128)(2,1)} %param.7) | copy-start | bytes 6291460
  7.2 433.0 %reduce-scatter.2.cloned.1.call-start = ((), (), s32[]{:S(2)}) async-start(), calls=%async_computation.2 | async-start | bytes 9437184 | tf_op jit(solution)/shard_map/reduce_scatter | solution.py:71
  29.6 1.6 copy-start.4
  32.3 125.8 %copy-start.2 = (bf16[256,2048]{1,0:T(8,128)(2,1)}, bf16[256,2048]{1,0:T(8,128)(2,1)S(1)}, u32[]{:S(2)}) copy-start(bf16[256,2048]{1,0:T(8,128)(2,1)S(1)} %get-tuple-element.22) | copy-start | bytes 3145732
  32.3 32.9 %collective-permute-start = (bf16[256,2048]{1,0:T(8,128)(2,1)S(1)}, bf16[256,2048]{1,0:T(8,128)(2,1)S(1)}, u32[]{:S(2)}, u32[]{:S(2)}) collective-permute-start(bf16[256,2048]{1,0:T(8,128)(2,1)S(1)} %get-tuple-element.22), channel_id=1, source_target_pairs={{0,7},{1,0},{2,1},{3,2},{4,3},{5,4},{6,5},{7,6},{8,15},{9,8},{10,9... | collective-permute-start | bytes 3145736 | tf_op jit(solution)/shard_map/ppermute | solution.py:21
  65.4 92.7 %collective-permute-start.1 = (bf16[512,2048]{1,0:T(8,128)(2,1)S(1)}, bf16[512,2048]{1,0:T(8,128)(2,1)S(1)}, u32[]{:S(2)}, u32[]{:S(2)}) collective-permute-start(bf16[512,2048]{1,0:T(8,128)(2,1)S(1)} %pad_maximum_fusion.1), channel_id=1, source_target_pairs={{0,6},{1,7},{2,0},{3,1},{4,2},{5,3},{6,4},{7,5},{8,14},{9,15},{10,... | collective-permute-start | bytes 6291464 | tf_op jit(solution)/shard_map/ppermute | solution.py:21
  160.4 190.8 %collective-permute-start.2 = (bf16[1024,2048]{1,0:T(8,128)(2,1)}, bf16[1024,2048]{1,0:T(8,128)(2,1)}, u32[]{:S(2)}, u32[]{:S(2)}) collective-permute-start(bf16[1024,2048]{1,0:T(8,128)(2,1)} %pad_maximum_fusion), channel_id=1, source_target_pairs={{0,4},{1,5},{2,6},{3,7},{4,0},{5,1},{6,2},{7,3},{8,12},{9,13},{10,... | collective-permute-start | bytes 12582920 | tf_op jit(solution)/shard_map/ppermute | solution.py:21
  163.0 193.0 %copy-start.3 = (bf16[256,2048]{1,0:T(8,128)(2,1)S(1)}, bf16[256,2048]{1,0:T(8,128)(2,1)}, u32[]{:S(2)}) copy-start(bf16[256,2048]{1,0:T(8,128)(2,1)} %copy-done.2) | copy-start | bytes 3145732
  359.5 4.9 %copy-start.10 = (bf16[1,1,512,2048]{3,2,1,0:T(8,128)(2,1)S(1)}, bf16[1,1,512,2048]{3,2,1,0:T(8,128)(2,1)}, u32[]{:S(2)}) copy-start(bf16[1,1,512,2048]{3,2,1,0:T(8,128)(2,1)} %param.8) | copy-start | bytes 6291460
  374.0 5.2 %copy-start.5 = (f32[256,2048]{1,0:T(8,128)S(1)}, f32[256,2048]{1,0:T(8,128)}, u32[]{:S(2)}) copy-start(f32[256,2048]{1,0:T(8,128)} %param.9) | copy-start | bytes 6291460
  374.0 53.0 %all-to-all-start = ((f32[4,128,2048]{2,1,0:T(8,128)}), f32[4,128,2048]{2,1,0:T(8,128)}, u32[]{:S(2)}, u32[]{:S(2)}) async-start(f32[4,128,2048]{2,1,0:T(8,128)} %fusion), calls=%async_computation | async-start | bytes 8388608 | tf_op jit(solution)/shard_map/all_to_all | solution.py:67
  379.2 2.0 copy-start.9
  381.5 3.0 copy-start.8
  434.0 6.2 %copy-start.6 = (f32[256,2048]{0,1:T(8,128)S(1)}, f32[256,2048]{0,1:T(8,128)}, u32[]{:S(2)}) copy-start(f32[256,2048]{0,1:T(8,128)} %copy.40) | copy-start | bytes 6291460
  446.5 3.0 copy-start.7
  451.3 3.0 copy-start.1
Sparse Core Ops, SparseCore 0:
  29.7 150.8 reduce-scatter.1
